TPU v7x, 256 devices: a whole 4x4x8 slice. The times are simulated.
256 devices in a mesh: grp: 4 (over y), dom: 64 (over x, z, core).
Axes of the slice: x: 4, y: 4, z: 8, core: 2. Of those that a mesh axis runs over, the one named last changes fastest.
Arguments:
- right_side: float32 [16, 524288], P(None, ('grp', 'dom')), may hold values from -38 to 38
- tile_values: float32 [24576, 128, 128], P(('grp', 'dom')), may hold values from 0 to 1, as said below
- tile_rows: int32 [24576], P(('grp', 'dom')), may hold values from 0 to 15
- tile_cols: int32 [24576], P(('grp', 'dom')), may hold values from 0 to 63, as said below
- tile_count: int32 [256], P(('grp', 'dom')), may hold values from 24 to 96, as said below
Outputs:
- solution_field: float32 [16, 524288], P(None, ('grp', 'dom'))
- residual: float32 [16, 524288], P(None, ('grp', 'dom'))
Inputs may be any that keep to these rules, and one draw needn't show every extreme that they name: `tile_cols`: values w * 16 + j name block j of the device just below along dom (w = 0), of the device itself (w = 1), of the device just above along dom (w = 2), or of the device of the same dom index whose grp index differs in the lowest bit (w = 3). No slot of a device at the first dom index names w = 0, none at the last names w = 2. `tile_count`: some device has all 96 slots live. `tile_values`: each row of a tile has at least one nonzero entry.
All inputs are finite; a program needn't handle non-finite values.
Results may differ from a plain program's by a relative error of at most 0.0003.
Values sent between devices are 32-bit elements; how exact they have to be, the bound alone decides.
No kernel may reach another device: no remote copies, remote signals or barrier semaphores. Data moves between devices by JAX's collectives and lax.ppermute only.
A program may use at most 64 MiB of HBM per device.

v0:
```python
import jax
import jax.numpy as jnp
from jax import lax
from jax.sharding import PartitionSpec as P

TILE = 128
NBD = 16
ITERS = 3


batch_slots = 8
damping = 0.8


def with_halo(shard, sides, width):
    for axis, dim in sides:
        size, length = (lax.axis_size(axis), shard.shape[dim])
        up = [(i, (i + 1) % size) for i in range(size - 1)]
        down = [(j, i) for i, j in up]
        last = lax.slice_in_dim(shard, length - width, length, axis=dim)
        initial = lax.slice_in_dim(shard, 0, width, axis=dim)
        before = lax.ppermute(last, axis, up)
        after = lax.ppermute(initial, axis, down)
        shard = jnp.concatenate([before, shard, after], axis=dim)
    return shard


def partner_2(value, axis, stride):
    mask = 2**stride
    pairs = [(source, source ^ mask) for source in range(lax.axis_size(axis))]
    return lax.ppermute(value, axis, pairs)


def to_blocks(field):
    rows_here, points_here = field.shape
    return field.reshape(rows_here, points_here // TILE, TILE).transpose(1, 0, 2)


def from_blocks(blocks):
    return blocks.transpose(1, 0, 2).reshape(blocks.shape[1], blocks.shape[0] * blocks.shape[2])


def fetch_window(scaled):
    shard_width = scaled.shape[1]
    padded = with_halo(scaled, (("dom", 1),), shard_width)
    partner = partner_2(scaled, "grp", 0)
    return to_blocks(jnp.concatenate([padded, partner], axis=1))


def any_window(columns):
    return columns >= 0


def tile_pass(tiles, tile_rows, tile_cols, live_count, window_blocks, own_blocks, wanted):
    own_total = own_blocks.shape[0]
    window_total = window_blocks.shape[0]
    slot_total = tiles.shape[0]
    slot_ids = jnp.arange(slot_total, dtype=jnp.int32)
    active = ((slot_ids < live_count) & wanted(tile_cols)).astype(jnp.float32)
    forward = jnp.einsum(
        "bij,bqj->bqi", tiles, window_blocks[tile_cols], precision=lax.Precision.HIGH
    )
    backward = jnp.einsum(
        "bij,bqi->bqj", tiles, own_blocks[tile_rows], precision=lax.Precision.HIGH
    )
    row_pick = (tile_rows[:, None] == jnp.arange(own_total, dtype=jnp.int32)[None, :]).astype(
        jnp.float32
    ) * active[:, None]
    col_pick = (tile_cols[:, None] == jnp.arange(window_total, dtype=jnp.int32)[None, :]).astype(
        jnp.float32
    ) * active[:, None]
    row_sums = jnp.einsum("bn,bqi->nqi", row_pick, forward, precision=lax.Precision.HIGHEST)
    window_sums = jnp.einsum("bn,bqi->nqi", col_pick, backward, precision=lax.Precision.HIGHEST)
    return (row_sums, window_sums)


def return_sums(row_sums, window_sums):
    shard_blocks = row_sums.shape[0]
    own_part = from_blocks(row_sums + window_sums[shard_blocks : 2 * shard_blocks])
    sideways = jnp.concatenate(
        [
            from_blocks(window_sums[:shard_blocks]),
            from_blocks(window_sums[2 * shard_blocks : 3 * shard_blocks]),
        ],
        axis=1,
    )
    shard_width = own_part.shape[1]
    returned = with_halo(sideways, (("dom", 1),), shard_width)
    across = partner_2(from_blocks(window_sums[3 * shard_blocks :]), "grp", 0)
    return own_part + returned[:, :shard_width] + returned[:, 3 * shard_width :] + across


def degrees(tiles, tile_rows, tile_cols, live_count):
    slot_total = tiles.shape[0]
    active = (jnp.arange(slot_total, dtype=jnp.int32) < live_count).astype(jnp.float32)
    row_pick = (tile_rows[:, None] == jnp.arange(NBD, dtype=jnp.int32)[None, :]).astype(
        jnp.float32
    ) * active[:, None]
    col_pick = (tile_cols[:, None] == jnp.arange(4 * NBD, dtype=jnp.int32)[None, :]).astype(
        jnp.float32
    ) * active[:, None]
    row_sums = jnp.einsum(
        "tn,ti->ni", row_pick, jnp.sum(tiles, axis=2), precision=lax.Precision.HIGHEST
    )[:, None, :]
    window_sums = jnp.einsum(
        "tn,ti->ni", col_pick, jnp.sum(tiles, axis=1), precision=lax.Precision.HIGHEST
    )[:, None, :]
    return 1.0 + return_sums(row_sums, window_sums)[0]


def apply_operator(field, point_scale, tiles, tile_rows, tile_cols, live_count):
    scaled = point_scale * field
    own_blocks = to_blocks(scaled)
    row_sums, window_sums = tile_pass(
        tiles, tile_rows, tile_cols, live_count, fetch_window(scaled), own_blocks, any_window
    )
    return field - damping * point_scale * return_sums(row_sums, window_sums)


def xor_sum(value, axes):
    for axis in axes:
        size = lax.axis_size(axis)
        stride = 1
        while stride < size:
            masks = [0]
            for step in (stride, 2 * stride):
                if step < size:
                    masks = masks + [mask ^ step for mask in masks]
            parts = [value] + [
                lax.ppermute(value, axis, [(i, i ^ mask) for i in range(size)]) for mask in masks[1:]
            ]
            while len(parts) > 1:
                parts = [parts[k] + parts[k + 1] for k in range(0, len(parts), 2)]
            value = parts[0]
            stride *= 4
    return value


def total(value):
    return xor_sum(value, ("dom", "grp"))


def squares(residual):
    return total(jnp.sum(residual * residual, axis=1))


def per_device(right_side, tile_values, tile_rows, tile_cols, tile_count):
    live_count = tile_count[0]
    point_scale = 1.0 / jnp.sqrt(degrees(tile_values, tile_rows, tile_cols, live_count))
    solution_field = jnp.zeros_like(right_side)
    residual = right_side
    direction = right_side
    norm_now = squares(residual)
    for iteration in range(ITERS):
        image = apply_operator(
            direction, point_scale, tile_values, tile_rows, tile_cols, live_count
        )
        curvature = total(jnp.sum(direction * image, axis=1))
        step_size = norm_now / curvature
        solution_field = solution_field + step_size[:, None] * direction
        residual = residual - step_size[:, None] * image
        norm_next = squares(residual)
        direction = residual + (norm_next / norm_now)[:, None] * direction
        norm_now = norm_next
    return (solution_field, residual)


def solution(mesh):
    placed = (
        P(None, ("grp", "dom")),
        P(("grp", "dom"), None, None),
        P(("grp", "dom")),
        P(("grp", "dom")),
        P(("grp", "dom")),
    )
    return jax.shard_map(
        per_device,
        mesh=mesh,
        in_specs=placed,
        out_specs=(P(None, ("grp", "dom")), P(None, ("grp", "dom"))),
        check_vma=False,
    )
```

profile of v0, /device:TPU:8, one launch (start us, length us, event | category | flops | bytes accessed | tf_op | source)
XLA Modules:
  0.0 271.3 jit_solution(9827751432190631268)
XLA Ops:
  1.3 4.5 %fusion.68 = (f32[96,128]{1,0:T(8,128)S(1)}, f32[96,128]{1,0:T(8,128)S(1)}) fusion(f32[96,128,128]{2,1,0:T(8,128)} %param.6), kind=kLoop, calls=%fused_computation.148 | loop fusion | flops 3121152 | bytes 6389760 | tf_op jit(solution)/shard_map/reduce_sum | solution.py:103
  16.1 4.7 %collective-permute-start.15 = (f32[16,2048]{1,0:T(8,128)S(1)}, f32[16,2048]{1,0:T(8,128)S(1)}, u32[]{:S(2)}, u32[]{:S(2)}) collective-permute-start(f32[16,2048]{1,0:T(8,128)S(1)} %broadcast_multiply_fusion.2), channel_id=1, source_target_pairs={{0,1},{1,2},{2,3},{3,4},{4,5},{5,6},{6,7},{7,8},{8,9},{9,10},{10,1... | collective-permute-start | bytes 393224 | tf_op jit(solution)/shard_map/ppermute | solution.py:22
  21.5 4.6 %fusion.79 = f32[96,16,128]{2,1,0:T(8,128)S(1)} fusion(f32[96,16,128]{2,1,0:T(8,128)S(1)} %gather_fusion.1, f32[96,128,128]{2,1,0:T(8,128)} %param.6), kind=kOutput, calls=%fused_computation.156 | convolution fusion | flops 150994944 | bytes 7864320 | tf_op jit(solution)/shard_map/bij,bqi->bqj/dot_general | solution.py:63
  28.9 4.0 %collective-permute-start.18 = (f32[16,2048]{1,0:T(8,128)S(1)}, f32[16,2048]{1,0:T(8,128)S(1)}, u32[]{:S(2)}, u32[]{:S(2)}) collective-permute-start(f32[16,2048]{1,0:T(8,128)S(1)} %bitcast.182), channel_id=1, source_target_pairs={{0,1},{1,2},{2,3},{3,4},{4,5},{5,6},{6,7},{7,8},{8,9},{9,10},{10,1... | collective-permute-start | bytes 393224 | tf_op jit(solution)/shard_map/ppermute | solution.py:22
  33.7 7.0 %fusion.78 = f32[96,16,128]{2,1,0:T(8,128)S(1)} fusion(f32[96,16,128]{2,1,0:T(8,128)S(1)} %gather_fusion, f32[96,128,128]{2,1,0:T(8,128)} %param.6), kind=kOutput, calls=%fused_computation.155 | convolution fusion | flops 150994944 | bytes 7864320 | tf_op jit(solution)/shard_map/bij,bqj->bqi/dot_general | solution.py:60
  41.6 3.6 %collective-permute-start.23 = (f32[16]{0:T(128)S(1)}, f32[16]{0:T(128)S(1)}, u32[]{:S(2)}, u32[]{:S(2)}) collective-permute-start(f32[16]{0:T(128)S(1)} %get-tuple-element.4), channel_id=1, source_target_pairs={{0,3},{1,2},{2,1},{3,0},{4,7},{5,6},{6,5},{7,4},{8,11},{9,10},{10,... | collective-permute-start | bytes 200 | tf_op jit(solution)/shard_map/ppermute | solution.py:130
  48.8 9.3 %collective-permute-start.26 = (f32[16]{0:T(128)S(1)}, f32[16]{0:T(128)S(1)}, u32[]{:S(2)}, u32[]{:S(2)}) collective-permute-start(f32[16]{0:T(128)S(1)} %add_add_fusion.16), channel_id=1, source_target_pairs={{0,12},{1,13},{2,14},{3,15},{4,8},{5,9},{6,10},{7,11},{8,4},{9,5},... | collective-permute-start | bytes 200 | tf_op jit(solution)/shard_map/ppermute | solution.py:130
  60.6 4.1 %collective-permute-start.5 = (f32[16]{0:T(128)S(1)}, f32[16]{0:T(128)S(1)}, u32[]{:S(2)}, u32[]{:S(2)}) collective-permute-start(f32[16]{0:T(128)S(1)} %add_add_fusion.20), channel_id=1, source_target_pairs={{0,12},{1,13},{2,14},{3,15},{4,8},{5,9},{6,10},{7,11},{8,4},{9,5},... | collective-permute-start | bytes 200 | tf_op jit(solution)/shard_map/ppermute | solution.py:130
  89.5 9.5 %collective-permute-start.33 = (f32[16]{0:T(128)S(1)}, f32[16]{0:T(128)S(1)}, u32[]{:S(2)}, u32[]{:S(2)}) collective-permute-start(f32[16]{0:T(128)S(1)} %multiply_reduce_fusion.3), channel_id=1, source_target_pairs={{0,1},{1,0},{2,3},{3,2},{4,5},{5,4},{6,7},{7,6},{8,9},{9,8},{10,11... | collective-permute-start | bytes 200 | tf_op jit(solution)/shard_map/ppermute | solution.py:130
  99.8 3.2 %collective-permute-start.38 = (f32[16]{0:T(128)S(1)}, f32[16]{0:T(128)S(1)}, u32[]{:S(2)}, u32[]{:S(2)}) collective-permute-start(f32[16]{0:T(128)S(1)} %add_add_fusion.13), channel_id=1, source_target_pairs={{0,12},{1,13},{2,14},{3,15},{4,8},{5,9},{6,10},{7,11},{8,4},{9,5},... | collective-permute-start | bytes 200 | tf_op jit(solution)/shard_map/ppermute | solution.py:130
  106.3 4.2 %collective-permute-done.37 = f32[16]{0:T(128)S(1)} collective-permute-done((f32[16]{0:T(128)S(1)}, f32[16]{0:T(128)S(1)}, u32[]{:S(2)}, u32[]{:S(2)}) %collective-permute-start.37) | collective-permute-done | bytes 96 | tf_op jit(solution)/shard_map/ppermute | solution.py:130
  127.6 3.0 %collective-permute-start.45 = (f32[16,2048]{1,0:T(8,128)S(1)}, f32[16,2048]{1,0:T(8,128)S(1)}, u32[]{:S(2)}, u32[]{:S(2)}) collective-permute-start(f32[16,2048]{1,0:T(8,128)S(1)} %get-tuple-element.16), channel_id=1, source_target_pairs={{0,1},{1,2},{2,3},{3,4},{4,5},{5,6},{6,7},{7,8},{8,9},{9,10},{10,1... | collective-permute-start | bytes 393224 | tf_op jit(solution)/shard_map/ppermute | solution.py:22
  131.4 4.6 %fusion.81 = f32[96,16,128]{2,1,0:T(8,128)S(1)} fusion(f32[96,16,128]{2,1,0:T(8,128)S(1)} %gather_fusion.3, f32[96,128,128]{2,1,0:T(8,128)} %param.6), kind=kOutput, calls=%fused_computation.158 | convolution fusion | flops 150994944 | bytes 7864320 | tf_op jit(solution)/shard_map/bij,bqi->bqj/dot_general | solution.py:63
  142.6 7.0 %fusion.80 = f32[96,16,128]{2,1,0:T(8,128)S(1)} fusion(f32[96,16,128]{2,1,0:T(8,128)S(1)} %gather_fusion.2, f32[96,128,128]{2,1,0:T(8,128)} %param.6), kind=kOutput, calls=%fused_computation.157 | convolution fusion | flops 150994944 | bytes 7864320 | tf_op jit(solution)/shard_map/bij,bqj->bqi/dot_general | solution.py:60
  156.6 6.0 %collective-permute-start.56 = (f32[16]{0:T(128)S(1)}, f32[16]{0:T(128)S(1)}, u32[]{:S(2)}, u32[]{:S(2)}) collective-permute-start(f32[16]{0:T(128)S(1)} %add_add_fusion.9), channel_id=1, source_target_pairs={{0,12},{1,13},{2,14},{3,15},{4,8},{5,9},{6,10},{7,11},{8,4},{9,5},... | collective-permute-start | bytes 200 | tf_op jit(solution)/shard_map/ppermute | solution.py:130
  165.0 5.0 %collective-permute-done.55 = f32[16]{0:T(128)S(1)} collective-permute-done((f32[16]{0:T(128)S(1)}, f32[16]{0:T(128)S(1)}, u32[]{:S(2)}, u32[]{:S(2)}) %collective-permute-start.55) | collective-permute-done | bytes 96 | tf_op jit(solution)/shard_map/ppermute | solution.py:130
  190.7 3.6 %collective-permute-start.66 = (f32[16]{0:T(128)S(1)}, f32[16]{0:T(128)S(1)}, u32[]{:S(2)}, u32[]{:S(2)}) collective-permute-start(f32[16]{0:T(128)S(1)} %add_add_fusion.6), channel_id=1, source_target_pairs={{0,4},{1,5},{2,6},{3,7},{4,0},{5,1},{6,2},{7,3},{8,12},{9,13},{10,... | collective-permute-start | bytes 200 | tf_op jit(solution)/shard_map/ppermute | solution.py:130
  213.0 3.0 %collective-permute-start.75 = (f32[16,2048]{1,0:T(8,128)S(1)}, f32[16,2048]{1,0:T(8,128)S(1)}, u32[]{:S(2)}, u32[]{:S(2)}) collective-permute-start(f32[16,2048]{1,0:T(8,128)S(1)} %get-tuple-element.8), channel_id=1, source_target_pairs={{0,1},{1,2},{2,3},{3,4},{4,5},{5,6},{6,7},{7,8},{8,9},{9,10},{10,1... | collective-permute-start | bytes 393224 | tf_op jit(solution)/shard_map/ppermute | solution.py:22
  216.9 4.6 %fusion.83 = f32[96,16,128]{2,1,0:T(8,128)S(1)} fusion(f32[96,16,128]{2,1,0:T(8,128)S(1)} %gather_fusion.5, f32[96,128,128]{2,1,0:T(8,128)} %param.6), kind=kOutput, calls=%fused_computation.160 | convolution fusion | flops 150994944 | bytes 7864320 | tf_op jit(solution)/shard_map/bij,bqi->bqj/dot_general | solution.py:63
  228.4 7.0 %fusion.82 = f32[96,16,128]{2,1,0:T(8,128)S(1)} fusion(f32[96,16,128]{2,1,0:T(8,128)S(1)} %gather_fusion.4, f32[96,128,128]{2,1,0:T(8,128)} %param.6), kind=kOutput, calls=%fused_computation.159 | convolution fusion | flops 150994944 | bytes 7864320 | tf_op jit(solution)/shard_map/bij,bqj->bqi/dot_general | solution.py:60
  237.0 4.3 %collective-permute-start.83 = (f32[16]{0:T(128)S(1)}, f32[16]{0:T(128)S(1)}, u32[]{:S(2)}, u32[]{:S(2)}) collective-permute-start(f32[16]{0:T(128)S(1)} %get-tuple-element.6), channel_id=1, source_target_pairs={{0,3},{1,2},{2,1},{3,0},{4,7},{5,6},{6,5},{7,4},{8,11},{9,10},{10,... | collective-permute-start | bytes 200 | tf_op jit(solution)/shard_map/ppermute | solution.py:130
  244.8 3.2 %collective-permute-start.86 = (f32[16]{0:T(128)S(1)}, f32[16]{0:T(128)S(1)}, u32[]{:S(2)}, u32[]{:S(2)}) collective-permute-start(f32[16]{0:T(128)S(1)} %add_add_fusion.2), channel_id=1, source_target_pairs={{0,12},{1,13},{2,14},{3,15},{4,8},{5,9},{6,10},{7,11},{8,4},{9,5},... | collective-permute-start | bytes 200 | tf_op jit(solution)/shard_map/ppermute | solution.py:130
  251.4 4.1 %collective-permute-done.85 = f32[16]{0:T(128)S(1)} collective-permute-done((f32[16]{0:T(128)S(1)}, f32[16]{0:T(128)S(1)}, u32[]{:S(2)}, u32[]{:S(2)}) %collective-permute-start.85) | collective-permute-done | bytes 96 | tf_op jit(solution)/shard_map/ppermute | solution.py:130
  255.9 3.4 %collective-permute-start.88 = (f32[16]{0:T(128)S(1)}, f32[16]{0:T(128)S(1)}, u32[]{:S(2)}, u32[]{:S(2)}) collective-permute-start(f32[16]{0:T(128)S(1)} %add_add_fusion.1), channel_id=1, source_target_pairs={{0,32},{1,33},{2,34},{3,35},{4,36},{5,37},{6,38},{7,39},{8,40},{9,... | collective-permute-start | bytes 200 | tf_op jit(solution)/shard_map/ppermute | solution.py:130
  (266 shorter events, 151.5 us)
Async XLA Ops:
  13.2 15.8 %collective-permute-start.17 = (f32[16,2048]{1,0:T(8,128)S(1)}, f32[16,2048]{1,0:T(8,128)S(1)}, u32[]{:S(2)}, u32[]{:S(2)}) collective-permute-start(f32[16,2048]{1,0:T(8,128)S(1)} %broadcast_multiply_fusion.2), channel_id=1, source_target_pairs={{0,64},{64,0},{128,192},{192,128},{1,65},{65,1},{129,193},{193,129... | collective-permute-start | bytes 393224 | tf_op jit(solution)/shard_map/ppermute | solution.py:31
  14.8 18.1 %collective-permute-start.16 = (f32[16,2048]{1,0:T(8,128)S(1)}, f32[16,2048]{1,0:T(8,128)S(1)}, u32[]{:S(2)}, u32[]{:S(2)}) collective-permute-start(f32[16,2048]{1,0:T(8,128)S(1)} %broadcast_multiply_fusion.2), channel_id=1, source_target_pairs={{1,0},{2,1},{3,2},{4,3},{5,4},{6,5},{7,6},{8,7},{9,8},{10,9},{11,1... | collective-permute-start | bytes 393224 | tf_op jit(solution)/shard_map/ppermute | solution.py:23
  16.1 16.8 %collective-permute-start.15 = (f32[16,2048]{1,0:T(8,128)S(1)}, f32[16,2048]{1,0:T(8,128)S(1)}, u32[]{:S(2)}, u32[]{:S(2)}) collective-permute-start(f32[16,2048]{1,0:T(8,128)S(1)} %broadcast_multiply_fusion.2), channel_id=1, source_target_pairs={{0,1},{1,2},{2,3},{3,4},{4,5},{5,6},{6,7},{7,8},{8,9},{9,10},{10,1... | collective-permute-start | bytes 393224 | tf_op jit(solution)/shard_map/ppermute | solution.py:22
  27.1 14.3 %collective-permute-start.19 = (f32[16,2048]{1,0:T(8,128)S(1)}, f32[16,2048]{1,0:T(8,128)S(1)}, u32[]{:S(2)}, u32[]{:S(2)}) collective-permute-start(f32[16,2048]{1,0:T(8,128)S(1)} %bitcast.188), channel_id=1, source_target_pairs={{1,0},{2,1},{3,2},{4,3},{5,4},{6,5},{7,6},{8,7},{9,8},{10,9},{11,1... | collective-permute-start | bytes 393224 | tf_op jit(solution)/shard_map/ppermute | solution.py:23
  28.4 13.0 %collective-permute-start.20 = (f32[16,2048]{1,0:T(8,128)S(1)}, f32[16,2048]{1,0:T(8,128)S(1)}, u32[]{:S(2)}, u32[]{:S(2)}) collective-permute-start(f32[16,2048]{1,0:T(8,128)S(1)} %bitcast.185), channel_id=1, source_target_pairs={{0,64},{64,0},{128,192},{192,128},{1,65},{65,1},{129,193},{193,129... | collective-permute-start | bytes 393224 | tf_op jit(solution)/shard_map/ppermute | solution.py:31
  28.9 12.5 %collective-permute-start.18 = (f32[16,2048]{1,0:T(8,128)S(1)}, f32[16,2048]{1,0:T(8,128)S(1)}, u32[]{:S(2)}, u32[]{:S(2)}) collective-permute-start(f32[16,2048]{1,0:T(8,128)S(1)} %bitcast.182), channel_id=1, source_target_pairs={{0,1},{1,2},{2,3},{3,4},{4,5},{5,6},{6,7},{7,8},{8,9},{9,10},{10,1... | collective-permute-start | bytes 393224 | tf_op jit(solution)/shard_map/ppermute | solution.py:22
  45.4 15.1 %collective-permute-start.2 = (f32[16]{0:T(128)S(1)}, f32[16]{0:T(128)S(1)}, u32[]{:S(2)}, u32[]{:S(2)}) collective-permute-start(f32[16]{0:T(128)S(1)} %get-tuple-element.5), channel_id=1, source_target_pairs={{0,3},{1,2},{2,1},{3,0},{4,7},{5,6},{6,5},{7,4},{8,11},{9,10},{10,... | collective-permute-start | bytes 200 | tf_op jit(solution)/shard_map/ppermute | solution.py:130
  47.4 13.3 %collective-permute-start.1 = (f32[16]{0:T(128)S(1)}, f32[16]{0:T(128)S(1)}, u32[]{:S(2)}, u32[]{:S(2)}) collective-permute-start(f32[16]{0:T(128)S(1)} %get-tuple-element.5), channel_id=1, source_target_pairs={{0,2},{1,3},{2,0},{3,1},{4,6},{5,7},{6,4},{7,5},{8,10},{9,11},{10,... | collective-permute-start | bytes 200 | tf_op jit(solution)/shard_map/ppermute | solution.py:130
  47.7 12.9 %collective-permute-start = (f32[16]{0:T(128)S(1)}, f32[16]{0:T(128)S(1)}, u32[]{:S(2)}, u32[]{:S(2)}) collective-permute-start(f32[16]{0:T(128)S(1)} %get-tuple-element.5), channel_id=1, source_target_pairs={{0,1},{1,0},{2,3},{3,2},{4,5},{5,4},{6,7},{7,6},{8,9},{9,8},{10,11... | collective-permute-start | bytes 200 | tf_op jit(solution)/shard_map/ppermute | solution.py:130
  48.8 18.4 %collective-permute-start.26 = (f32[16]{0:T(128)S(1)}, f32[16]{0:T(128)S(1)}, u32[]{:S(2)}, u32[]{:S(2)}) collective-permute-start(f32[16]{0:T(128)S(1)} %add_add_fusion.16), channel_id=1, source_target_pairs={{0,12},{1,13},{2,14},{3,15},{4,8},{5,9},{6,10},{7,11},{8,4},{9,5},... | collective-permute-start | bytes 200 | tf_op jit(solution)/shard_map/ppermute | solution.py:130
  88.4 10.5 %collective-permute-start.35 = (f32[16]{0:T(128)S(1)}, f32[16]{0:T(128)S(1)}, u32[]{:S(2)}, u32[]{:S(2)}) collective-permute-start(f32[16]{0:T(128)S(1)} %multiply_reduce_fusion.3), channel_id=1, source_target_pairs={{0,3},{1,2},{2,1},{3,0},{4,7},{5,6},{6,5},{7,4},{8,11},{9,10},{10,... | collective-permute-start | bytes 200 | tf_op jit(solution)/shard_map/ppermute | solution.py:130
  88.5 10.4 %collective-permute-start.34 = (f32[16]{0:T(128)S(1)}, f32[16]{0:T(128)S(1)}, u32[]{:S(2)}, u32[]{:S(2)}) collective-permute-start(f32[16]{0:T(128)S(1)} %multiply_reduce_fusion.3), channel_id=1, source_target_pairs={{0,2},{1,3},{2,0},{3,1},{4,6},{5,7},{6,4},{7,5},{8,10},{9,11},{10,... | collective-permute-start | bytes 200 | tf_op jit(solution)/shard_map/ppermute | solution.py:130
  124.9 14.2 %collective-permute-start.47 = (f32[16,2048]{1,0:T(8,128)S(1)}, f32[16,2048]{1,0:T(8,128)S(1)}, u32[]{:S(2)}, u32[]{:S(2)}) collective-permute-start(f32[16,2048]{1,0:T(8,128)S(1)} %get-tuple-element.16), channel_id=1, source_target_pairs={{0,64},{64,0},{128,192},{192,128},{1,65},{65,1},{129,193},{193,129... | collective-permute-start | bytes 393224 | tf_op jit(solution)/shard_map/ppermute | solution.py:31
  126.3 15.5 %collective-permute-start.46 = (f32[16,2048]{1,0:T(8,128)S(1)}, f32[16,2048]{1,0:T(8,128)S(1)}, u32[]{:S(2)}, u32[]{:S(2)}) collective-permute-start(f32[16,2048]{1,0:T(8,128)S(1)} %get-tuple-element.16), channel_id=1, source_target_pairs={{1,0},{2,1},{3,2},{4,3},{5,4},{6,5},{7,6},{8,7},{9,8},{10,9},{11,1... | collective-permute-start | bytes 393224 | tf_op jit(solution)/shard_map/ppermute | solution.py:23
  127.6 14.3 %collective-permute-start.45 = (f32[16,2048]{1,0:T(8,128)S(1)}, f32[16,2048]{1,0:T(8,128)S(1)}, u32[]{:S(2)}, u32[]{:S(2)}) collective-permute-start(f32[16,2048]{1,0:T(8,128)S(1)} %get-tuple-element.16), channel_id=1, source_target_pairs={{0,1},{1,2},{2,3},{3,4},{4,5},{5,6},{6,7},{7,8},{8,9},{9,10},{10,1... | collective-permute-start | bytes 393224 | tf_op jit(solution)/shard_map/ppermute | solution.py:22
  137.0 13.4 %collective-permute-start.49 = (f32[16,2048]{1,0:T(8,128)S(1)}, f32[16,2048]{1,0:T(8,128)S(1)}, u32[]{:S(2)}, u32[]{:S(2)}) collective-permute-start(f32[16,2048]{1,0:T(8,128)S(1)} %bitcast.189), channel_id=1, source_target_pairs={{1,0},{2,1},{3,2},{4,3},{5,4},{6,5},{7,6},{8,7},{9,8},{10,9},{11,1... | collective-permute-start | bytes 393224 | tf_op jit(solution)/shard_map/ppermute | solution.py:23
  138.3 12.1 %collective-permute-start.50 = (f32[16,2048]{1,0:T(8,128)S(1)}, f32[16,2048]{1,0:T(8,128)S(1)}, u32[]{:S(2)}, u32[]{:S(2)}) collective-permute-start(f32[16,2048]{1,0:T(8,128)S(1)} %bitcast.186), channel_id=1, source_target_pairs={{0,64},{64,0},{128,192},{192,128},{1,65},{65,1},{129,193},{193,129... | collective-permute-start | bytes 393224 | tf_op jit(solution)/shard_map/ppermute | solution.py:31
  139.1 11.3 %collective-permute-start.48 = (f32[16,2048]{1,0:T(8,128)S(1)}, f32[16,2048]{1,0:T(8,128)S(1)}, u32[]{:S(2)}, u32[]{:S(2)}) collective-permute-start(f32[16,2048]{1,0:T(8,128)S(1)} %bitcast.183), channel_id=1, source_target_pairs={{0,1},{1,2},{2,3},{3,4},{4,5},{5,6},{6,7},{7,8},{8,9},{9,10},{10,1... | collective-permute-start | bytes 393224 | tf_op jit(solution)/shard_map/ppermute | solution.py:22
  210.4 14.3 %collective-permute-start.77 = (f32[16,2048]{1,0:T(8,128)S(1)}, f32[16,2048]{1,0:T(8,128)S(1)}, u32[]{:S(2)}, u32[]{:S(2)}) collective-permute-start(f32[16,2048]{1,0:T(8,128)S(1)} %get-tuple-element.8), channel_id=1, source_target_pairs={{0,64},{64,0},{128,192},{192,128},{1,65},{65,1},{129,193},{193,129... | collective-permute-start | bytes 393224 | tf_op jit(solution)/shard_map/ppermute | solution.py:31
  211.7 15.8 %collective-permute-start.76 = (f32[16,2048]{1,0:T(8,128)S(1)}, f32[16,2048]{1,0:T(8,128)S(1)}, u32[]{:S(2)}, u32[]{:S(2)}) collective-permute-start(f32[16,2048]{1,0:T(8,128)S(1)} %get-tuple-element.8), channel_id=1, source_target_pairs={{1,0},{2,1},{3,2},{4,3},{5,4},{6,5},{7,6},{8,7},{9,8},{10,9},{11,1... | collective-permute-start | bytes 393224 | tf_op jit(solution)/shard_map/ppermute | solution.py:23
  213.0 14.5 %collective-permute-start.75 = (f32[16,2048]{1,0:T(8,128)S(1)}, f32[16,2048]{1,0:T(8,128)S(1)}, u32[]{:S(2)}, u32[]{:S(2)}) collective-permute-start(f32[16,2048]{1,0:T(8,128)S(1)} %get-tuple-element.8), channel_id=1, source_target_pairs={{0,1},{1,2},{2,3},{3,4},{4,5},{5,6},{6,7},{7,8},{8,9},{9,10},{10,1... | collective-permute-start | bytes 393224 | tf_op jit(solution)/shard_map/ppermute | solution.py:22
  222.5 14.2 %collective-permute-start.79 = (f32[16,2048]{1,0:T(8,128)S(1)}, f32[16,2048]{1,0:T(8,128)S(1)}, u32[]{:S(2)}, u32[]{:S(2)}) collective-permute-start(f32[16,2048]{1,0:T(8,128)S(1)} %bitcast.187), channel_id=1, source_target_pairs={{1,0},{2,1},{3,2},{4,3},{5,4},{6,5},{7,6},{8,7},{9,8},{10,9},{11,1... | collective-permute-start | bytes 393224 | tf_op jit(solution)/shard_map/ppermute | solution.py:23
  223.8 13.0 %collective-permute-start.80 = (f32[16,2048]{1,0:T(8,128)S(1)}, f32[16,2048]{1,0:T(8,128)S(1)}, u32[]{:S(2)}, u32[]{:S(2)}) collective-permute-start(f32[16,2048]{1,0:T(8,128)S(1)} %bitcast.184), channel_id=1, source_target_pairs={{0,64},{64,0},{128,192},{192,128},{1,65},{65,1},{129,193},{193,129... | collective-permute-start | bytes 393224 | tf_op jit(solution)/shard_map/ppermute | solution.py:31
  224.7 12.0 %collective-permute-start.78 = (f32[16,2048]{1,0:T(8,128)S(1)}, f32[16,2048]{1,0:T(8,128)S(1)}, u32[]{:S(2)}, u32[]{:S(2)}) collective-permute-start(f32[16,2048]{1,0:T(8,128)S(1)} %bitcast.181), channel_id=1, source_target_pairs={{0,1},{1,2},{2,3},{3,4},{4,5},{5,6},{6,7},{7,8},{8,9},{9,10},{10,1... | collective-permute-start | bytes 393224 | tf_op jit(solution)/shard_map/ppermute | solution.py:22
  (82 other events, 1169.4 us)
where the time goes:
time: 276 us; the launch traced here: 271 us
  starting transfers between devices  164 us (59%)
  waiting for transfers between devices  52.2 us (19%)
  matrix products  40.3 us (15%)
  other arithmetic  8 us (3%)
  local copies, waits for them, and re-layouts  4.97 us (2%)
    ppermute x72, starting transfers between devices, xor_sum(): lax.ppermute(value, axis, [(i, i ^ mask) for i in range(size)])  124 us
    ppermute x72, waiting for transfers between devices, xor_sum(): lax.ppermute(value, axis, [(i, i ^ mask) for i in range(size)])  50.2 us
    ppermute x7, starting transfers between devices, with_halo(): before = lax.ppermute(last, axis, up)  21.5 us
    dot_general x3, matrix products, tile_pass(): jnp.einsum('bij,bqj->bqi', tiles, window_blocks[tile_cols], precision=lax...  21 us
    dot_general x3, matrix products, tile_pass(): jnp.einsum('bij,bqi->bqj', tiles, own_blocks[tile_rows], precision=lax.Pr...  13.7 us
    ppermute x7, starting transfers between devices, with_halo(): after = lax.ppermute(initial, axis, down)  9.01 us
    ppermute x7, starting transfers between devices, partner_2(): return lax.ppermute(value, axis, pairs)  8.84 us
  transfers between devices with their start and end apart: 93, of which 33 were waited for; matrix products, arithmetic and copies ran while one was open for 17% of the time, Pallas kernels for 0%

commit v1 on v0

--- a/solution.py
+++ b/solution.py
@@ -151,16 +151,21 @@
     residual = right_side
     direction = right_side
     norm_now = squares(residual)
+    image = apply_operator(direction, point_scale, tile_values, tile_rows, tile_cols, live_count)
     for iteration in range(ITERS):
-        image = apply_operator(
-            direction, point_scale, tile_values, tile_rows, tile_cols, live_count
-        )
         curvature = total(jnp.sum(direction * image, axis=1))
         step_size = norm_now / curvature
         solution_field = solution_field + step_size[:, None] * direction
         residual = residual - step_size[:, None] * image
+        if iteration + 1 == ITERS:
+            break
         norm_next = squares(residual)
-        direction = residual + (norm_next / norm_now)[:, None] * direction
+        residual_image = apply_operator(
+            residual, point_scale, tile_values, tile_rows, tile_cols, live_count
+        )
+        growth = (norm_next / norm_now)[:, None]
+        direction = residual + growth * direction
+        image = residual_image + growth * image
         norm_now = norm_next
     return (solution_field, residual)
 

time: 276 us -> 287 us (1.040)
  waiting for transfers between devices: 52.2 us -> 57.4 us
  starting transfers between devices: 164 us -> 168 us
    ppermute x72, starting transfers between devices: 124 us -> 132 us  [xor_sum(): lax.ppermute(value, axis, [(i, i ^ mask) for i in range(size)])]
    ppermute x7, starting transfers between devices: 21.5 us -> 15.6 us  [with_halo(): before = lax.ppermute(last, axis, up)]
    ppermute x72, waiting for transfers between devices: 50.2 us -> 55.6 us  [xor_sum(): lax.ppermute(value, axis, [(i, i ^ mask) for i in range(size)])]
    ppermute x7, starting transfers between devices: 8.84 us -> 11.9 us  [partner_2(): return lax.ppermute(value, axis, pairs)]
  transfers between devices with their start and end apart: 93 -> 93, of which waited for: 33 -> 40; matrix products, arithmetic and copies ran while one was open for 17% -> 16% of each run, Pallas kernels for 0% -> 0%
where the time goes in v1:
time: 287 us; the launch traced here: 282 us
  starting transfers between devices  168 us (59%)
  waiting for transfers between devices  57.4 us (20%)
  matrix products  39.6 us (14%)
  other arithmetic  9.3 us (3%)
  local copies, waits for them, and re-layouts  5.56 us (2%)
    ppermute x72, starting transfers between devices, xor_sum(): lax.ppermute(value, axis, [(i, i ^ mask) for i in range(size)])  132 us
    ppermute x72, waiting for transfers between devices, xor_sum(): lax.ppermute(value, axis, [(i, i ^ mask) for i in range(size)])  55.6 us
    dot_general x3, matrix products, tile_pass(): jnp.einsum('bij,bqj->bqi', tiles, window_blocks[tile_cols], precision=lax...  21 us
    ppermute x7, starting transfers between devices, with_halo(): before = lax.ppermute(last, axis, up)  15.6 us
    dot_general x3, matrix products, tile_pass(): jnp.einsum('bij,bqi->bqj', tiles, own_blocks[tile_rows], precision=lax.Pr...  13.7 us
    ppermute x7, starting transfers between devices, partner_2(): return lax.ppermute(value, axis, pairs)  11.9 us
    ppermute x7, starting transfers between devices, with_halo(): after = lax.ppermute(initial, axis, down)  9.02 us
  transfers between devices with their start and end apart: 93, of which 40 were waited for; matrix products, arithmetic and copies ran while one was open for 16% of the time, Pallas kernels for 0%

profile of v1, /device:TPU:8, one launch (start us, length us, event | category | flops | bytes accessed | tf_op | source)
XLA Modules:
  0.0 282.3 jit_solution(16178763101619511554)
XLA Ops:
  1.3 4.5 %fusion.70 = (f32[96,128]{1,0:T(8,128)S(1)}, f32[96,128]{1,0:T(8,128)S(1)}) fusion(f32[96,128,128]{2,1,0:T(8,128)} %param.6), kind=kLoop, calls=%fused_computation.150 | loop fusion | flops 3121152 | bytes 6389760 | tf_op jit(solution)/shard_map/reduce_sum | solution.py:103
  12.9 4.0 %collective-permute-start.15 = (f32[16,2048]{1,0:T(8,128)S(1)}, f32[16,2048]{1,0:T(8,128)S(1)}, u32[]{:S(2)}, u32[]{:S(2)}) collective-permute-start(f32[16,2048]{1,0:T(8,128)S(1)} %broadcast_multiply_fusion.2), channel_id=1, source_target_pairs={{0,1},{1,2},{2,3},{3,4},{4,5},{5,6},{6,7},{7,8},{8,9},{9,10},{10,1... | collective-permute-start | bytes 393224 | tf_op jit(solution)/shard_map/ppermute | solution.py:22
  19.5 4.6 %fusion.81 = f32[96,16,128]{2,1,0:T(8,128)S(1)} fusion(f32[96,16,128]{2,1,0:T(8,128)S(1)} %gather_fusion.1, f32[96,128,128]{2,1,0:T(8,128)} %param.6), kind=kOutput, calls=%fused_computation.158 | convolution fusion | flops 150994944 | bytes 7864320 | tf_op jit(solution)/shard_map/bij,bqi->bqj/dot_general | solution.py:63
  25.0 4.7 %collective-permute-start.18 = (f32[16,2048]{1,0:T(8,128)S(1)}, f32[16,2048]{1,0:T(8,128)S(1)}, u32[]{:S(2)}, u32[]{:S(2)}) collective-permute-start(f32[16,2048]{1,0:T(8,128)S(1)} %bitcast.192), channel_id=1, source_target_pairs={{0,1},{1,2},{2,3},{3,4},{4,5},{5,6},{6,7},{7,8},{8,9},{9,10},{10,1... | collective-permute-start | bytes 393224 | tf_op jit(solution)/shard_map/ppermute | solution.py:22
  33.5 7.0 %fusion.80 = f32[96,16,128]{2,1,0:T(8,128)S(1)} fusion(f32[96,16,128]{2,1,0:T(8,128)S(1)} %gather_fusion, f32[96,128,128]{2,1,0:T(8,128)} %param.6), kind=kOutput, calls=%fused_computation.157 | convolution fusion | flops 150994944 | bytes 7864320 | tf_op jit(solution)/shard_map/bij,bqj->bqi/dot_general | solution.py:60
  48.9 6.8 %collective-permute-start.3 = (f32[16]{0:T(128)S(1)}, f32[16]{0:T(128)S(1)}, u32[]{:S(2)}, u32[]{:S(2)}) collective-permute-start(f32[16]{0:T(128)S(1)} %add_add_fusion.20), channel_id=1, source_target_pairs={{0,4},{1,5},{2,6},{3,7},{4,0},{5,1},{6,2},{7,3},{8,12},{9,13},{10,... | collective-permute-start | bytes 200 | tf_op jit(solution)/shard_map/ppermute | solution.py:130
  55.7 3.1 %collective-permute-start.4 = (f32[16]{0:T(128)S(1)}, f32[16]{0:T(128)S(1)}, u32[]{:S(2)}, u32[]{:S(2)}) collective-permute-start(f32[16]{0:T(128)S(1)} %add_add_fusion.20), channel_id=1, source_target_pairs={{0,8},{1,9},{2,10},{3,11},{4,12},{5,13},{6,14},{7,15},{8,0},{9,1},... | collective-permute-start | bytes 200 | tf_op jit(solution)/shard_map/ppermute | solution.py:130
  62.3 3.1 %collective-permute-start.25 = (f32[16]{0:T(128)S(1)}, f32[16]{0:T(128)S(1)}, u32[]{:S(2)}, u32[]{:S(2)}) collective-permute-start(f32[16]{0:T(128)S(1)} %add_add_fusion.16), channel_id=1, source_target_pairs={{0,8},{1,9},{2,10},{3,11},{4,12},{5,13},{6,14},{7,15},{8,0},{9,1},... | collective-permute-start | bytes 200 | tf_op jit(solution)/shard_map/ppermute | solution.py:130
  66.0 4.4 %collective-permute-start.6 = (f32[16]{0:T(128)S(1)}, f32[16]{0:T(128)S(1)}, u32[]{:S(2)}, u32[]{:S(2)}) collective-permute-start(f32[16]{0:T(128)S(1)} %add_add_fusion.19), channel_id=1, source_target_pairs={{0,16},{1,17},{2,18},{3,19},{4,20},{5,21},{6,22},{7,23},{8,24},{9,... | collective-permute-start | bytes 200 | tf_op jit(solution)/shard_map/ppermute | solution.py:130
  74.0 4.2 %collective-permute-start.28 = (f32[16]{0:T(128)S(1)}, f32[16]{0:T(128)S(1)}, u32[]{:S(2)}, u32[]{:S(2)}) collective-permute-start(f32[16]{0:T(128)S(1)} %add_add_fusion.15), channel_id=1, source_target_pairs={{0,32},{1,33},{2,34},{3,35},{4,36},{5,37},{6,38},{7,39},{8,40},{9,... | collective-permute-start | bytes 200 | tf_op jit(solution)/shard_map/ppermute | solution.py:130
  97.9 10.9 %collective-permute-start.34 = (f32[16]{0:T(128)S(1)}, f32[16]{0:T(128)S(1)}, u32[]{:S(2)}, u32[]{:S(2)}) collective-permute-start(f32[16]{0:T(128)S(1)} %get-tuple-element.16), channel_id=1, source_target_pairs={{0,2},{1,3},{2,0},{3,1},{4,6},{5,7},{6,4},{7,5},{8,10},{9,11},{10,... | collective-permute-start | bytes 200 | tf_op jit(solution)/shard_map/ppermute | solution.py:130
  109.5 4.6 %fusion.83 = f32[96,16,128]{2,1,0:T(8,128)S(1)} fusion(f32[96,16,128]{2,1,0:T(8,128)S(1)} %gather_fusion.3, f32[96,128,128]{2,1,0:T(8,128)} %param.6), kind=kOutput, calls=%fused_computation.160 | convolution fusion | flops 150994944 | bytes 7864320 | tf_op jit(solution)/shard_map/bij,bqi->bqj/dot_general | solution.py:63
  128.3 4.7 %collective-permute-start.40 = (f32[16]{0:T(128)S(1)}, f32[16]{0:T(128)S(1)}, u32[]{:S(2)}, u32[]{:S(2)}) collective-permute-start(f32[16]{0:T(128)S(1)} %add_add_fusion.12), channel_id=1, source_target_pairs={{0,32},{1,33},{2,34},{3,35},{4,36},{5,37},{6,38},{7,39},{8,40},{9,... | collective-permute-start | bytes 200 | tf_op jit(solution)/shard_map/ppermute | solution.py:130
  148.5 7.0 %fusion.82 = f32[96,16,128]{2,1,0:T(8,128)S(1)} fusion(f32[96,16,128]{2,1,0:T(8,128)S(1)} %gather_fusion.2, f32[96,128,128]{2,1,0:T(8,128)} %param.6), kind=kOutput, calls=%fused_computation.159 | convolution fusion | flops 150994944 | bytes 7864320 | tf_op jit(solution)/shard_map/bij,bqj->bqi/dot_general | solution.py:60
  165.3 4.0 %collective-permute-start.55 = (f32[16]{0:T(128)S(1)}, f32[16]{0:T(128)S(1)}, u32[]{:S(2)}, u32[]{:S(2)}) collective-permute-start(f32[16]{0:T(128)S(1)} %add_add_fusion.9), channel_id=1, source_target_pairs={{0,8},{1,9},{2,10},{3,11},{4,12},{5,13},{6,14},{7,15},{8,0},{9,1},... | collective-permute-start | bytes 200 | tf_op jit(solution)/shard_map/ppermute | solution.py:130
  175.0 3.6 %collective-permute-start.58 = (f32[16]{0:T(128)S(1)}, f32[16]{0:T(128)S(1)}, u32[]{:S(2)}, u32[]{:S(2)}) collective-permute-start(f32[16]{0:T(128)S(1)} %add_add_fusion.8), channel_id=1, source_target_pairs={{0,32},{1,33},{2,34},{3,35},{4,36},{5,37},{6,38},{7,39},{8,40},{9,... | collective-permute-start | bytes 200 | tf_op jit(solution)/shard_map/ppermute | solution.py:130
  180.2 3.2 %collective-permute-done.59 = f32[16]{0:T(128)S(1)} collective-permute-done((f32[16]{0:T(128)S(1)}, f32[16]{0:T(128)S(1)}, u32[]{:S(2)}, u32[]{:S(2)}) %collective-permute-start.59) | collective-permute-done | bytes 96 | tf_op jit(solution)/shard_map/ppermute | solution.py:130
  198.9 4.6 %fusion.85 = f32[96,16,128]{2,1,0:T(8,128)S(1)} fusion(f32[96,16,128]{2,1,0:T(8,128)S(1)} %gather_fusion.5, f32[96,128,128]{2,1,0:T(8,128)} %param.6), kind=kOutput, calls=%fused_computation.162 | convolution fusion | flops 150994944 | bytes 7864320 | tf_op jit(solution)/shard_map/bij,bqi->bqj/dot_general | solution.py:63
  209.5 4.0 %collective-permute-start.67 = (f32[16]{0:T(128)S(1)}, f32[16]{0:T(128)S(1)}, u32[]{:S(2)}, u32[]{:S(2)}) collective-permute-start(f32[16]{0:T(128)S(1)} %add_add_fusion.6), channel_id=1, source_target_pairs={{0,8},{1,9},{2,10},{3,11},{4,12},{5,13},{6,14},{7,15},{8,0},{9,1},... | collective-permute-start | bytes 200 | tf_op jit(solution)/shard_map/ppermute | solution.py:130
  224.5 3.2 %collective-permute-done.71 = f32[16]{0:T(128)S(1)} collective-permute-done((f32[16]{0:T(128)S(1)}, f32[16]{0:T(128)S(1)}, u32[]{:S(2)}, u32[]{:S(2)}) %collective-permute-start.71) | collective-permute-done | bytes 96 | tf_op jit(solution)/shard_map/ppermute | solution.py:130
  239.2 7.0 %fusion.84 = f32[96,16,128]{2,1,0:T(8,128)S(1)} fusion(f32[96,16,128]{2,1,0:T(8,128)S(1)} %gather_fusion.4, f32[96,128,128]{2,1,0:T(8,128)} %param.6), kind=kOutput, calls=%fused_computation.161 | convolution fusion | flops 150994944 | bytes 7864320 | tf_op jit(solution)/shard_map/bij,bqj->bqi/dot_general | solution.py:60
  255.8 3.4 %collective-permute-start.85 = (f32[16]{0:T(128)S(1)}, f32[16]{0:T(128)S(1)}, u32[]{:S(2)}, u32[]{:S(2)}) collective-permute-start(f32[16]{0:T(128)S(1)} %add_add_fusion.2), channel_id=1, source_target_pairs={{0,8},{1,9},{2,10},{3,11},{4,12},{5,13},{6,14},{7,15},{8,0},{9,1},... | collective-permute-start | bytes 200 | tf_op jit(solution)/shard_map/ppermute | solution.py:130
  265.0 3.6 %collective-permute-start.88 = (f32[16]{0:T(128)S(1)}, f32[16]{0:T(128)S(1)}, u32[]{:S(2)}, u32[]{:S(2)}) collective-permute-start(f32[16]{0:T(128)S(1)} %add_add_fusion.1), channel_id=1, source_target_pairs={{0,32},{1,33},{2,34},{3,35},{4,36},{5,37},{6,38},{7,39},{8,40},{9,... | collective-permute-start | bytes 200 | tf_op jit(solution)/shard_map/ppermute | solution.py:130
  270.1 3.2 %collective-permute-done.89 = f32[16]{0:T(128)S(1)} collective-permute-done((f32[16]{0:T(128)S(1)}, f32[16]{0:T(128)S(1)}, u32[]{:S(2)}, u32[]{:S(2)}) %collective-permute-start.89) | collective-permute-done | bytes 96 | tf_op jit(solution)/shard_map/ppermute | solution.py:130
  (272 shorter events, 166.4 us)
Async XLA Ops:
  12.9 18.2 %collective-permute-start.15 = (f32[16,2048]{1,0:T(8,128)S(1)}, f32[16,2048]{1,0:T(8,128)S(1)}, u32[]{:S(2)}, u32[]{:S(2)}) collective-permute-start(f32[16,2048]{1,0:T(8,128)S(1)} %broadcast_multiply_fusion.2), channel_id=1, source_target_pairs={{0,1},{1,2},{2,3},{3,4},{4,5},{5,6},{6,7},{7,8},{8,9},{9,10},{10,1... | collective-permute-start | bytes 393224 | tf_op jit(solution)/shard_map/ppermute | solution.py:22
  17.0 15.8 %collective-permute-start.16 = (f32[16,2048]{1,0:T(8,128)S(1)}, f32[16,2048]{1,0:T(8,128)S(1)}, u32[]{:S(2)}, u32[]{:S(2)}) collective-permute-start(f32[16,2048]{1,0:T(8,128)S(1)} %broadcast_multiply_fusion.2), channel_id=1, source_target_pairs={{1,0},{2,1},{3,2},{4,3},{5,4},{6,5},{7,6},{8,7},{9,8},{10,9},{11,1... | collective-permute-start | bytes 393224 | tf_op jit(solution)/shard_map/ppermute | solution.py:23
  18.3 14.5 %collective-permute-start.17 = (f32[16,2048]{1,0:T(8,128)S(1)}, f32[16,2048]{1,0:T(8,128)S(1)}, u32[]{:S(2)}, u32[]{:S(2)}) collective-permute-start(f32[16,2048]{1,0:T(8,128)S(1)} %broadcast_multiply_fusion.2), channel_id=1, source_target_pairs={{0,64},{64,0},{128,192},{192,128},{1,65},{65,1},{129,193},{193,129... | collective-permute-start | bytes 393224 | tf_op jit(solution)/shard_map/ppermute | solution.py:31
  25.0 16.2 %collective-permute-start.18 = (f32[16,2048]{1,0:T(8,128)S(1)}, f32[16,2048]{1,0:T(8,128)S(1)}, u32[]{:S(2)}, u32[]{:S(2)}) collective-permute-start(f32[16,2048]{1,0:T(8,128)S(1)} %bitcast.192), channel_id=1, source_target_pairs={{0,1},{1,2},{2,3},{3,4},{4,5},{5,6},{6,7},{7,8},{8,9},{9,10},{10,1... | collective-permute-start | bytes 393224 | tf_op jit(solution)/shard_map/ppermute | solution.py:22
  29.8 11.5 %collective-permute-start.19 = (f32[16,2048]{1,0:T(8,128)S(1)}, f32[16,2048]{1,0:T(8,128)S(1)}, u32[]{:S(2)}, u32[]{:S(2)}) collective-permute-start(f32[16,2048]{1,0:T(8,128)S(1)} %bitcast.193), channel_id=1, source_target_pairs={{1,0},{2,1},{3,2},{4,3},{5,4},{6,5},{7,6},{8,7},{9,8},{10,9},{11,1... | collective-permute-start | bytes 393224 | tf_op jit(solution)/shard_map/ppermute | solution.py:23
  45.9 13.0 %collective-permute-start.21 = (f32[16]{0:T(128)S(1)}, f32[16]{0:T(128)S(1)}, u32[]{:S(2)}, u32[]{:S(2)}) collective-permute-start(f32[16]{0:T(128)S(1)} %get-tuple-element.4), channel_id=1, source_target_pairs={{0,1},{1,0},{2,3},{3,2},{4,5},{5,4},{6,7},{7,6},{8,9},{9,8},{10,11... | collective-permute-start | bytes 200 | tf_op jit(solution)/shard_map/ppermute | solution.py:130
  46.1 13.3 %collective-permute-start.22 = (f32[16]{0:T(128)S(1)}, f32[16]{0:T(128)S(1)}, u32[]{:S(2)}, u32[]{:S(2)}) collective-permute-start(f32[16]{0:T(128)S(1)} %get-tuple-element.4), channel_id=1, source_target_pairs={{0,2},{1,3},{2,0},{3,1},{4,6},{5,7},{6,4},{7,5},{8,10},{9,11},{10,... | collective-permute-start | bytes 200 | tf_op jit(solution)/shard_map/ppermute | solution.py:130
  48.3 11.1 %collective-permute-start.23 = (f32[16]{0:T(128)S(1)}, f32[16]{0:T(128)S(1)}, u32[]{:S(2)}, u32[]{:S(2)}) collective-permute-start(f32[16]{0:T(128)S(1)} %get-tuple-element.4), channel_id=1, source_target_pairs={{0,3},{1,2},{2,1},{3,0},{4,7},{5,6},{6,5},{7,4},{8,11},{9,10},{10,... | collective-permute-start | bytes 200 | tf_op jit(solution)/shard_map/ppermute | solution.py:130
  48.9 16.6 %collective-permute-start.3 = (f32[16]{0:T(128)S(1)}, f32[16]{0:T(128)S(1)}, u32[]{:S(2)}, u32[]{:S(2)}) collective-permute-start(f32[16]{0:T(128)S(1)} %add_add_fusion.20), channel_id=1, source_target_pairs={{0,4},{1,5},{2,6},{3,7},{4,0},{5,1},{6,2},{7,3},{8,12},{9,13},{10,... | collective-permute-start | bytes 200 | tf_op jit(solution)/shard_map/ppermute | solution.py:130
  59.4 14.0 %collective-permute-start.24 = (f32[16]{0:T(128)S(1)}, f32[16]{0:T(128)S(1)}, u32[]{:S(2)}, u32[]{:S(2)}) collective-permute-start(f32[16]{0:T(128)S(1)} %add_add_fusion.16), channel_id=1, source_target_pairs={{0,4},{1,5},{2,6},{3,7},{4,0},{5,1},{6,2},{7,3},{8,12},{9,13},{10,... | collective-permute-start | bytes 200 | tf_op jit(solution)/shard_map/ppermute | solution.py:130
  62.3 11.1 %collective-permute-start.25 = (f32[16]{0:T(128)S(1)}, f32[16]{0:T(128)S(1)}, u32[]{:S(2)}, u32[]{:S(2)}) collective-permute-start(f32[16]{0:T(128)S(1)} %add_add_fusion.16), channel_id=1, source_target_pairs={{0,8},{1,9},{2,10},{3,11},{4,12},{5,13},{6,14},{7,15},{8,0},{9,1},... | collective-permute-start | bytes 200 | tf_op jit(solution)/shard_map/ppermute | solution.py:130
  66.0 12.2 %collective-permute-start.6 = (f32[16]{0:T(128)S(1)}, f32[16]{0:T(128)S(1)}, u32[]{:S(2)}, u32[]{:S(2)}) collective-permute-start(f32[16]{0:T(128)S(1)} %add_add_fusion.19), channel_id=1, source_target_pairs={{0,16},{1,17},{2,18},{3,19},{4,20},{5,21},{6,22},{7,23},{8,24},{9,... | collective-permute-start | bytes 200 | tf_op jit(solution)/shard_map/ppermute | solution.py:130
  90.0 56.3 %collective-permute-start.45 = (f32[16,2048]{1,0:T(8,128)S(1)}, f32[16,2048]{1,0:T(8,128)S(1)}, u32[]{:S(2)}, u32[]{:S(2)}) collective-permute-start(f32[16,2048]{1,0:T(8,128)S(1)} %broadcast_multiply_fusion.1), channel_id=1, source_target_pairs={{0,1},{1,2},{2,3},{3,4},{4,5},{5,6},{6,7},{7,8},{8,9},{9,10},{10,1... | collective-permute-start | bytes 393224 | tf_op jit(solution)/shard_map/ppermute | solution.py:22
  91.3 56.4 %collective-permute-start.46 = (f32[16,2048]{1,0:T(8,128)S(1)}, f32[16,2048]{1,0:T(8,128)S(1)}, u32[]{:S(2)}, u32[]{:S(2)}) collective-permute-start(f32[16,2048]{1,0:T(8,128)S(1)} %broadcast_multiply_fusion.1), channel_id=1, source_target_pairs={{1,0},{2,1},{3,2},{4,3},{5,4},{6,5},{7,6},{8,7},{9,8},{10,9},{11,1... | collective-permute-start | bytes 393224 | tf_op jit(solution)/shard_map/ppermute | solution.py:23
  92.6 55.1 %collective-permute-start.47 = (f32[16,2048]{1,0:T(8,128)S(1)}, f32[16,2048]{1,0:T(8,128)S(1)}, u32[]{:S(2)}, u32[]{:S(2)}) collective-permute-start(f32[16,2048]{1,0:T(8,128)S(1)} %broadcast_multiply_fusion.1), channel_id=1, source_target_pairs={{0,64},{64,0},{128,192},{192,128},{1,65},{65,1},{129,193},{193,129... | collective-permute-start | bytes 393224 | tf_op jit(solution)/shard_map/ppermute | solution.py:31
  95.7 19.4 %collective-permute-start.33 = (f32[16]{0:T(128)S(1)}, f32[16]{0:T(128)S(1)}, u32[]{:S(2)}, u32[]{:S(2)}) collective-permute-start(f32[16]{0:T(128)S(1)} %get-tuple-element.16), channel_id=1, source_target_pairs={{0,1},{1,0},{2,3},{3,2},{4,5},{5,4},{6,7},{7,6},{8,9},{9,8},{10,11... | collective-permute-start | bytes 200 | tf_op jit(solution)/shard_map/ppermute | solution.py:130
  97.9 17.3 %collective-permute-start.34 = (f32[16]{0:T(128)S(1)}, f32[16]{0:T(128)S(1)}, u32[]{:S(2)}, u32[]{:S(2)}) collective-permute-start(f32[16]{0:T(128)S(1)} %get-tuple-element.16), channel_id=1, source_target_pairs={{0,2},{1,3},{2,0},{3,1},{4,6},{5,7},{6,4},{7,5},{8,10},{9,11},{10,... | collective-permute-start | bytes 200 | tf_op jit(solution)/shard_map/ppermute | solution.py:130
  143.0 13.2 %collective-permute-start.48 = (f32[16,2048]{1,0:T(8,128)S(1)}, f32[16,2048]{1,0:T(8,128)S(1)}, u32[]{:S(2)}, u32[]{:S(2)}) collective-permute-start(f32[16,2048]{1,0:T(8,128)S(1)} %bitcast.191), channel_id=1, source_target_pairs={{0,1},{1,2},{2,3},{3,4},{4,5},{5,6},{6,7},{7,8},{8,9},{9,10},{10,1... | collective-permute-start | bytes 393224 | tf_op jit(solution)/shard_map/ppermute | solution.py:22
  145.0 11.2 %collective-permute-start.49 = (f32[16,2048]{1,0:T(8,128)S(1)}, f32[16,2048]{1,0:T(8,128)S(1)}, u32[]{:S(2)}, u32[]{:S(2)}) collective-permute-start(f32[16,2048]{1,0:T(8,128)S(1)} %bitcast.189), channel_id=1, source_target_pairs={{1,0},{2,1},{3,2},{4,3},{5,4},{6,5},{7,6},{8,7},{9,8},{10,9},{11,1... | collective-permute-start | bytes 393224 | tf_op jit(solution)/shard_map/ppermute | solution.py:23
  189.5 47.3 %collective-permute-start.75 = (f32[16,2048]{1,0:T(8,128)S(1)}, f32[16,2048]{1,0:T(8,128)S(1)}, u32[]{:S(2)}, u32[]{:S(2)}) collective-permute-start(f32[16,2048]{1,0:T(8,128)S(1)} %get-tuple-element.10), channel_id=1, source_target_pairs={{0,1},{1,2},{2,3},{3,4},{4,5},{5,6},{6,7},{7,8},{8,9},{9,10},{10,1... | collective-permute-start | bytes 393224 | tf_op jit(solution)/shard_map/ppermute | solution.py:22
  190.8 47.4 %collective-permute-start.76 = (f32[16,2048]{1,0:T(8,128)S(1)}, f32[16,2048]{1,0:T(8,128)S(1)}, u32[]{:S(2)}, u32[]{:S(2)}) collective-permute-start(f32[16,2048]{1,0:T(8,128)S(1)} %get-tuple-element.10), channel_id=1, source_target_pairs={{1,0},{2,1},{3,2},{4,3},{5,4},{6,5},{7,6},{8,7},{9,8},{10,9},{11,1... | collective-permute-start | bytes 393224 | tf_op jit(solution)/shard_map/ppermute | solution.py:23
  192.1 46.1 %collective-permute-start.77 = (f32[16,2048]{1,0:T(8,128)S(1)}, f32[16,2048]{1,0:T(8,128)S(1)}, u32[]{:S(2)}, u32[]{:S(2)}) collective-permute-start(f32[16,2048]{1,0:T(8,128)S(1)} %get-tuple-element.10), channel_id=1, source_target_pairs={{0,64},{64,0},{128,192},{192,128},{1,65},{65,1},{129,193},{193,129... | collective-permute-start | bytes 393224 | tf_op jit(solution)/shard_map/ppermute | solution.py:31
  232.9 14.0 %collective-permute-start.78 = (f32[16,2048]{1,0:T(8,128)S(1)}, f32[16,2048]{1,0:T(8,128)S(1)}, u32[]{:S(2)}, u32[]{:S(2)}) collective-permute-start(f32[16,2048]{1,0:T(8,128)S(1)} %bitcast.190), channel_id=1, source_target_pairs={{0,1},{1,2},{2,3},{3,4},{4,5},{5,6},{6,7},{7,8},{8,9},{9,10},{10,1... | collective-permute-start | bytes 393224 | tf_op jit(solution)/shard_map/ppermute | solution.py:22
  234.9 12.0 %collective-permute-start.79 = (f32[16,2048]{1,0:T(8,128)S(1)}, f32[16,2048]{1,0:T(8,128)S(1)}, u32[]{:S(2)}, u32[]{:S(2)}) collective-permute-start(f32[16,2048]{1,0:T(8,128)S(1)} %bitcast.188), channel_id=1, source_target_pairs={{1,0},{2,1},{3,2},{4,3},{5,4},{6,5},{7,6},{8,7},{9,8},{10,9},{11,1... | collective-permute-start | bytes 393224 | tf_op jit(solution)/shard_map/ppermute | solution.py:23
  (85 other events, 1134.2 us)
